TPU v7x, 32 devices: a whole 2x2x4 slice. The times are simulated.
32 devices in a mesh: groups: 2 (over y), space: 8 (over z, x), tm: 2 (over core).
Axes of the slice: x: 2, y: 2, z: 4, core: 2. Of those that a mesh axis runs over, the one named last changes fastest.
Arguments:
- latents: bfloat16 [4, 16, 4, 256, 256], P('groups', 'space', 'tm'), parts along dimension 0, may hold values from -6 to 6
- cotangent: bfloat16 [4, 16, 4, 256, 256], P('groups', 'space', 'tm'), parts along dimension 0, may hold values from -6 to 6
- valid_frames: int32 [4], P('groups'), parts along dimension 0, may hold values from 1 to 16, as said below
- spatial_weight: bfloat16 [9, 256, 256], replicated, may hold values from -0.125 to 0.125
- temporal_weight: bfloat16 [3, 256, 256], replicated, may hold values from -0.21875 to 0.21875
- cond_weight: bfloat16 [256, 256], replicated, may hold values from -0.375 to 0.375
Outputs:
- output: bfloat16 [4, 16, 4, 256, 256], P('groups', 'space', 'tm'), parts along dimension 0
- grad_latents: bfloat16 [4, 16, 4, 256, 256], P('groups', 'space', 'tm'), parts along dimension 0
- grad_spatial: bfloat16 [18, 256, 256], P('groups'), parts along dimension 0
- grad_temporal: bfloat16 [6, 256, 256], P('groups'), parts along dimension 0
- grad_cond: bfloat16 [512, 256], P('groups'), parts along dimension 0
There are 2 independent parts, one for each index of `groups`. A program takes and returns all parts, laid end to end along the dimension named above; an argument that names none is the same for every part. Nothing has to cross between parts.
Inputs may be any that keep to these rules, and one draw needn't show every extreme that they name: `valid_frames`: the first clip has all 16 frames valid; the others have 1 to 16.
All inputs are finite; a program needn't handle non-finite values.
Results may differ from a plain program's by a relative error of at most 0.0055.
Values may be sent and summed in bfloat16 or wider, within the bound.
No kernel may reach another device: no remote copies, remote signals or barrier semaphores. Data moves between devices by JAX's collectives and lax.ppermute only.
A program may use at most 128 MiB of HBM per device.

v0:
```python
import jax
import jax.numpy as jnp
from jax import lax
from jax.sharding import PartitionSpec as P


def from_root(block, axis, source):
    block = jnp.where(lax.axis_index(axis) == source, block, jnp.zeros_like(block))
    return lax.psum(block, axis)


def shifted(value, axis, by):
    count = lax.axis_size(axis)
    pairs = [(i, i + by) for i in range(count) if 0 <= i + by < count]
    return lax.ppermute(value, axis, pairs)


def spatial_sum(padded, weights, flip):
    rows = padded.shape[2] - 2
    cols = padded.shape[3] - 2
    total = jnp.zeros(padded.shape[:2] + (rows, cols, weights.shape[2]), jnp.float32)
    for row_off in range(3):
        for col_off in range(3):
            if flip:
                piece = padded[
                    :, :, 2 - row_off : 2 - row_off + rows, 2 - col_off : 2 - col_off + cols
                ]
                kernel = weights[3 * row_off + col_off].T
            else:
                piece = padded[:, :, row_off : row_off + rows, col_off : col_off + cols]
                kernel = weights[3 * row_off + col_off]
            total = total + jnp.dot(piece, kernel, preferred_element_type=jnp.float32)
    return total


def lag_forward(padded_act, weights, count):
    total = 0.0
    for lag in range(3):
        total = total + jnp.dot(
            padded_act[:, 2 - lag : 2 - lag + count],
            weights[lag],
            preferred_element_type=jnp.float32,
        )
    return total


def lag_backward(padded_cot, weights, count):
    total = 0.0
    for lag in range(3):
        total = total + jnp.dot(
            padded_cot[:, lag : lag + count], weights[lag].T, preferred_element_type=jnp.float32
        )
    return total


def lag_grads(padded_act, cot, count):
    dims = (((0, 1, 2, 3), (0, 1, 2, 3)), ((), ()))
    terms = []
    for lag in range(3):
        terms.append(
            lax.dot_general(
                padded_act[:, 2 - lag : 2 - lag + count],
                cot,
                dims,
                preferred_element_type=jnp.float32,
            )
        )
    return jnp.stack(terms)


def own_window(whole, rows):
    padded_rows = jnp.pad(whole, ((0, 0), (0, 0), (1, 1), (0, 0), (0, 0)))
    start = lax.axis_index("tm") * rows
    return lax.dynamic_slice_in_dim(padded_rows, start, rows + 2, 2)


def on_device(latents, cotangent, valid_frames, spatial_weight, temporal_weight, cond_weight):
    clips, frames, rows, cols, chans = latents.shape
    slab = lax.axis_index("space")
    frame_ids = slab * frames + jnp.arange(frames, dtype=jnp.int32)
    mask = (frame_ids[None, :] < valid_frames[:, None]).astype(jnp.bfloat16)[:, :, None, None, None]
    mask_f = mask.astype(jnp.float32)
    masked = latents * mask
    first = from_root(masked[:, 0], "space", 0)
    rows_pad = own_window(lax.all_gather(masked, "tm", axis=2, tiled=True), rows)
    padded = jnp.pad(rows_pad, ((0, 0), (0, 0), (0, 0), (1, 1), (0, 0)))
    pre = spatial_sum(padded, spatial_weight, False)
    act = jax.nn.silu(pre).astype(jnp.bfloat16)
    cot = cotangent * mask
    earlier = shifted(act, "space", 1)
    act_pad = jnp.concatenate([earlier, act], axis=1)
    mixed = lag_forward(act_pad, temporal_weight, frames)
    later = shifted(cot, "space", -1)
    cot_pad = jnp.concatenate([cot, later], axis=1)
    dact = lag_backward(cot_pad, temporal_weight, frames)
    temporal_terms = lag_grads(act_pad, cot, frames)
    cond = jnp.dot(first, cond_weight, preferred_element_type=jnp.float32)
    output = ((masked.astype(jnp.float32) + mixed + cond[:, None]) * mask_f).astype(jnp.bfloat16)
    sig = jax.nn.sigmoid(pre)
    dpre = (dact * sig * (1.0 + pre * (1.0 - sig))).astype(jnp.bfloat16)
    cot_sum = lax.psum(jnp.sum(cot, axis=1, dtype=jnp.float32), "space")
    cond_back = jnp.dot(cot_sum, cond_weight.astype(jnp.float32).T, precision=lax.Precision.HIGHEST)
    dpre_rows = own_window(lax.all_gather(dpre, "tm", axis=2, tiled=True), rows)
    dpre_pad = jnp.pad(dpre_rows, ((0, 0), (0, 0), (0, 0), (1, 1), (0, 0)))
    dmasked = spatial_sum(dpre_pad, spatial_weight, True)
    is_first = (frame_ids == 0).astype(jnp.float32)[None, :, None, None, None]
    grad_latents = (
        (cot.astype(jnp.float32) + dmasked + is_first * cond_back[:, None]) * mask_f
    ).astype(jnp.bfloat16)
    dims = (((0, 1, 2, 3), (0, 1, 2, 3)), ((), ()))
    spatial_terms = []
    for row_off in range(3):
        for col_off in range(3):
            piece = padded[:, :, row_off : row_off + rows, col_off : col_off + cols]
            spatial_terms.append(
                lax.dot_general(piece, dpre, dims, preferred_element_type=jnp.float32)
            )
    spatial_terms = jnp.stack(spatial_terms)
    is_owner = (slab == 0).astype(jnp.float32)
    cond_terms = is_owner * lax.dot_general(
        first.astype(jnp.float32),
        cot_sum,
        (((0, 1, 2), (0, 1, 2)), ((), ())),
        precision=lax.Precision.HIGHEST,
    )
    summed = lax.psum((spatial_terms, temporal_terms, cond_terms), ("space", "tm"))
    scale = (clips * frames * rows * cols * lax.axis_size("space") * lax.axis_size("tm")) ** (-0.5)
    grad_spatial = (summed[0] * scale).astype(jnp.bfloat16)
    grad_temporal = (summed[1] * scale).astype(jnp.bfloat16)
    grad_cond = (summed[2] * scale).astype(jnp.bfloat16)
    return (output, grad_latents, grad_spatial, grad_temporal, grad_cond)


def solution(mesh):
    return jax.shard_map(
        on_device,
        mesh=mesh,
        in_specs=(
            P("groups", "space", "tm", None, None),
            P("groups", "space", "tm", None, None),
            P("groups"),
            P(),
            P(),
            P(),
        ),
        out_specs=(
            P("groups", "space", "tm", None, None),
            P("groups", "space", "tm", None, None),
            P("groups", None, None),
            P("groups", None, None),
            P("groups", None),
        ),
        check_vma=False,
    )
```

profile of v0, /device:TPU:0, one launch (start us, length us, event | category | flops | bytes accessed | tf_op | source)
XLA Modules:
  0.0 338.7 jit_solution(10557166967447815481)
XLA Ops:
  8.1 0.7 fusion.124
  8.8 1.4 broadcast_multiply_fusion.1
  10.2 0.9 fusion.44
  11.2 2.7 convert_reduce_fusion
  14.0 0.5 all-gather.3.cloned.1.call-update
  14.5 1.3 collective-permute-start.1
  15.9 1.8 fusion.75
  17.7 75.7 %all-reduce.9.cloned.1.call-done = bf16[2,2,256,256]{3,2,1,0:T(8,128)(2,1)} async-done(((bf16[2,2,256,256]{3,2,1,0:T(8,128)(2,1)}), bf16[2,2,256,256]{3,2,1,0:T(8,128)(2,1)}) %all-reduce.9.cloned.1.call-update) | async-done | bytes 524304 | tf_op jit(solution)/shard_map/psum | solution.py:9
  93.3 2.3 fusion.47
  95.7 79.6 %all-reduce.11.cloned.1.call-done = f32[2,2,256,256]{3,2,1,0:T(8,128)} async-done(((f32[2,2,256,256]{3,2,1,0:T(8,128)}), f32[2,2,256,256]{3,2,1,0:T(8,128)}) %all-reduce.11.cloned.1.call-update) | async-done | bytes 1048592 | tf_op jit(solution)/shard_map/psum | solution.py:101
  175.3 3.0 fusion.13
  178.2 1.6 fusion.45
  179.9 1.8 fusion.3
  181.7 1.8 pad_dynamic-slice_fusion.1
  187.1 2.1 multiply_convert_fusion.3
  189.4 0.5 copy-done.24
  189.9 2.0 multiply_convert_fusion.1
  191.9 1.2 fusion.19
  193.2 3.5 %collective-permute-start = (bf16[2,2,2,256,256]{4,3,2,1,0:T(8,128)(2,1)}, bf16[2,2,2,256,256]{4,3,2,1,0:T(8,128)(2,1)S(1)}, u32[]{:S(2)}, u32[]{:S(2)}) collective-permute-start(bf16[2,2,2,256,256]{4,3,2,1,0:T(8,128)(2,1)} %get-tuple-element.12), channel_id=1, source_target_pairs={{0,2},{2,4},{4,6},{6,8},{8,10},{10,12},{12,14},{1,3},{3,5},{5,7},{... | collective-permute-start | bytes 3145736 | tf_op jit(solution)/shard_map/ppermute | solution.py:15
  196.7 2.4 fusion.12
  199.1 1.2 fusion.18
  200.3 1.2 fusion.17
  201.5 1.2 fusion.11
  202.7 1.2 fusion.16
  203.8 1.2 fusion.15
  205.9 1.2 fusion.10
  207.1 1.2 fusion.14
  208.3 2.7 fusion.77
  211.0 7.8 %collective-permute-done = bf16[2,2,2,256,256]{4,3,2,1,0:T(8,128)(2,1)S(1)} collective-permute-done((bf16[2,2,2,256,256]{4,3,2,1,0:T(8,128)(2,1)}, bf16[2,2,2,256,256]{4,3,2,1,0:T(8,128)(2,1)S(1)}, u32[]{:S(2)}, u32[]{:S(2)}) %collective-permute-start) | collective-permute-done | bytes 1048608 | tf_op jit(solution)/shard_map/ppermute | solution.py:15
  219.3 0.5 fusion.9
  219.8 1.0 pad_maximum_fusion.5
  220.8 1.2 copy-done.8
  222.9 0.8 copy-done.12
  223.7 0.7 copy-done.13
  224.6 1.7 multiply_convert_fusion.2
  226.3 1.8 pad_dynamic-slice_fusion
  228.2 0.5 fusion.20
  228.6 0.5 fusion.22
  229.1 0.5 fusion.24
  229.6 0.5 fusion.26
  230.1 0.5 fusion.28
  230.6 0.5 fusion.30
  232.0 0.8 copy-done.6
  233.1 2.2 fusion.2
  235.3 91.7 %all-reduce.13.cloned.1.call-done = (f32[9,256,256]{2,1,0:T(8,128)}, f32[3,256,256]{2,1,0:T(8,128)}, f32[256,256]{1,0:T(8,128)}) async-done(((f32[9,256,256]{2,1,0:T(8,128)}, f32[3,256,256]{2,1,0:T(8,128)}, f32[256,256]{1,0:T(8,128)}), (f32[9,256,256]{2,1,0:T(8,128)}, f32[3,256,256]{2,1,0:T(8,128)}, f32[256,256]{1,0:T(8,128)})) %all-reduce.13.cloned.1.call-update) | async-done | bytes 3407888 | tf_op jit(solution)/shard_map/psum | solution.py:126
  327.0 3.0 multiply_convert_fusion
  330.0 0.8 multiply_convert_fusion.4
  330.9 0.7 multiply_convert_fusion.5
  (76 shorter events, 7.8 us)
Async XLA Ops:
  8.0 85.3 %copy-start = (bf16[256,256]{1,0:T(8,128)(2,1)S(1)}, bf16[256,256]{1,0:T(8,128)(2,1)}, u32[]{:S(2)}) copy-start(bf16[256,256]{1,0:T(8,128)(2,1)} %param.11) | copy-start | bytes 393220
  8.0 85.3 %all-reduce.9.cloned.1.call-start = ((), (), s32[]{:S(2)}) async-start(), calls=%async_computation.1 | async-start | bytes 1048576 | tf_op jit(solution)/shard_map/psum | solution.py:9
  10.2 3.7 %copy-start.11 = (bf16[2,2,2,256,256]{4,3,2,1,0:T(8,128)(2,1)}, bf16[2,2,2,256,256]{4,3,2,1,0:T(8,128)(2,1)S(1)}, u32[]{:S(2)}) copy-start(bf16[2,2,2,256,256]{4,3,2,1,0:T(8,128)(2,1)S(1)} %broadcast_multiply_fusion.1) | copy-start | bytes 3145732
  11.1 4.8 %copy-start.21 = (bf16[3,256,256]{2,1,0:T(8,128)(2,1)S(1)}, bf16[3,256,256]{2,1,0:T(8,128)(2,1)}, u32[]{:S(2)}) copy-start(bf16[3,256,256]{2,1,0:T(8,128)(2,1)} %param.10) | copy-start | bytes 1179652
  11.1 164.2 %all-reduce.11.cloned.1.call-start = ((), (), s32[]{:S(2)}) async-start(), calls=%async_computation.3 | async-start | bytes 2097152 | tf_op jit(solution)/shard_map/psum | solution.py:101
  13.9 166.0 %copy-start.4 = (bf16[2,2,2,256,256]{4,3,2,1,0:T(8,128)(2,1)}, bf16[2,2,2,256,256]{4,3,2,1,0:T(8,128)(2,1)S(1)}, u32[]{:S(2)}) copy-start(bf16[2,2,2,256,256]{4,3,2,1,0:T(8,128)(2,1)S(1)} %get-tuple-element.9) | copy-start | bytes 3145732
  13.9 167.8 %all-gather.3.cloned.1.call-start = ((), (), s32[]{:S(2)}) async-start(), calls=%async_computation | async-start | bytes 3145728 | tf_op jit(solution)/shard_map/all_gather | solution.py:85
  14.5 211.8 %all-gather.5.cloned.1.call-start = ((), (), s32[]{:S(2)}) async-start(), calls=%async_computation.2 | async-start | bytes 3145728 | tf_op jit(solution)/shard_map/all_gather | solution.py:103
  14.5 165.3 %collective-permute-start.1 = (bf16[2,2,2,256,256]{4,3,2,1,0:T(8,128)(2,1)S(1)}, bf16[2,2,2,256,256]{4,3,2,1,0:T(8,128)(2,1)S(1)}, u32[]{:S(2)}, u32[]{:S(2)}) collective-permute-start(bf16[2,2,2,256,256]{4,3,2,1,0:T(8,128)(2,1)S(1)} %get-tuple-element.9), channel_id=1, source_target_pairs={{2,0},{4,2},{6,4},{8,6},{10,8},{12,10},{14,12},{3,1},{5,3},{7,5},{... | collective-permute-start | bytes 3145736 | tf_op jit(solution)/shard_map/ppermute | solution.py:15
  175.3 3.0 copy-start.18
  179.8 1.8 copy-start.23
  181.7 1.8 copy-start.14
  187.1 2.2 copy-start.19
  187.1 2.3 copy-start.20
  187.1 2.8 copy-start.24
  191.9 1.2 copy-start.2
  193.1 6.0 %copy-start.3 = (bf16[2,2,2,256,256]{4,3,2,1,0:T(8,128)(2,1)S(1)}, bf16[2,2,2,256,256]{4,3,2,1,0:T(8,128)(2,1)}, u32[]{:S(2)}) copy-start(bf16[2,2,2,256,256]{4,3,2,1,0:T(8,128)(2,1)} %copy-done.2) | copy-start | bytes 3145732
  193.2 133.8 %all-reduce.13.cloned.1.call-start = ((), (), s32[]{:S(2)}) async-start(), calls=%async_computation.4 | async-start | bytes 6815744 | tf_op jit(solution)/shard_map/psum | solution.py:126
  193.2 25.7 %collective-permute-start = (bf16[2,2,2,256,256]{4,3,2,1,0:T(8,128)(2,1)}, bf16[2,2,2,256,256]{4,3,2,1,0:T(8,128)(2,1)S(1)}, u32[]{:S(2)}, u32[]{:S(2)}) collective-permute-start(bf16[2,2,2,256,256]{4,3,2,1,0:T(8,128)(2,1)} %get-tuple-element.12), channel_id=1, source_target_pairs={{0,2},{2,4},{4,6},{6,8},{8,10},{10,12},{12,14},{1,3},{3,5},{5,7},{... | collective-permute-start | bytes 3145736 | tf_op jit(solution)/shard_map/ppermute | solution.py:15
  203.8 1.2 copy-start.5
  203.8 1.6 copy-start.7
  218.9 1.0 copy-start.9
  220.8 1.2 copy-start.8
  220.8 1.5 copy-start.10
  220.8 1.6 copy-start.22
  222.4 1.2 copy-start.12
  222.4 1.9 copy-start.13
  222.4 2.2 copy-start.17
  226.3 1.9 copy-start.15
  231.6 1.2 copy-start.6
  231.6 1.6 copy-start.16
  327.0 3.0 copy-start.25
  327.0 4.5 %copy-start.1 = (bf16[256,256]{1,0:T(8,128)(2,1)S(1)}, bf16[256,256]{1,0:T(8,128)(2,1)}, u32[]{:S(2)}) copy-start(bf16[256,256]{1,0:T(8,128)(2,1)} %param.11) | copy-start | bytes 393220
  327.0 3.9 %copy-start.26 = (f32[256,256]{1,0:T(8,128)S(1)}, f32[256,256]{1,0:T(8,128)}, u32[]{:S(2)}) copy-start(f32[256,256]{1,0:T(8,128)} %get-tuple-element.7) | copy-start | bytes 786436
Sparse Core Ops, SparseCore 0:
  12.8 80.4 all-reduce.8
  97.8 77.4 all-reduce.10
  220.9 105.9 all-reduce.12
Sparse Core Ops, SparseCore 1:
  16.5 13.1 all-gather.2
  193.2 10.0 all-gather.4
where the time goes:
time: 339 us
  waiting for transfers between devices  255 us (75%)
  matrix products  42.3 us (12%)
  between operations  15.5 us (5%)
  other arithmetic  11.2 us (3%)
  local copies, waits for them, and re-layouts  9.27 us (3%)
  starting transfers between devices  5.03 us (1%)
    psum x1, waiting for transfers between devices, on_device(): lax.psum((spatial_terms, temporal_terms, cond_terms), ('space', 'tm'))  91.7 us
    psum x1, waiting for transfers between devices, on_device(): cot_sum = lax.psum(jnp.sum(cot, axis=1, dtype=jnp.float32), 'space')  79.6 us
    psum x1, waiting for transfers between devices, from_root(): return lax.psum(block, axis)  75.7 us
    dot_general x9, matrix products, on_device(): lax.dot_general(piece, dpre, dims, preferred_element_type=jnp.float32)  11.9 us
    dot_general x18, matrix products, spatial_sum(): total = total + jnp.dot(piece, kernel, preferred_element_type=jnp.float32)  11.7 us
    ppermute x2, waiting for transfers between devices, shifted(): return lax.ppermute(value, axis, pairs)  7.84 us
  transfers between devices with their start and end apart: 7, of which 4 were waited for; matrix products, arithmetic and copies ran while one was open for 12% of the time, Pallas kernels for 0%

commit v1 on v0

--- a/solution.py
+++ b/solution.py
@@ -4,9 +4,13 @@
 from jax.sharding import PartitionSpec as P
 
 
+def work_pairs_all(tile_in, mesh_ax):
+    return jax.lax.all_gather(tile_in, mesh_ax).sum(axis=0)
+
+
 def from_root(block, axis, source):
     block = jnp.where(lax.axis_index(axis) == source, block, jnp.zeros_like(block))
-    return lax.psum(block, axis)
+    return work_pairs_all(block, axis)
 
 
 def shifted(value, axis, by):

time: 339 us -> 320 us (0.944)
  waiting for transfers between devices: 255 us -> 222 us
  matrix products: 42.3 us -> 52.1 us
  other arithmetic: 11.2 us -> 14.9 us
    psum x1 -> x0, waiting for transfers between devices: 75.7 us -> none  [from_root(): return lax.psum(block, axis)]
    ppermute x2, waiting for transfers between devices: 7.84 us -> 60.3 us  [shifted(): return lax.ppermute(value, axis, pairs)]
    psum x1, waiting for transfers between devices: 79.6 us -> 61 us  [on_device(): cot_sum = lax.psum(jnp.sum(cot, axis=1, dtype=jnp.float32), 'space')]
    dot_general x18, matrix products: 11.7 us -> 28.7 us  [spatial_sum(): total = total + jnp.dot(piece, kernel, preferred_element_type=jnp.float32)]
    psum x1, waiting for transfers between devices: 91.7 us -> 101 us  [on_device(): lax.psum((spatial_terms, temporal_terms, cond_terms), ('space', 'tm'))]
    dot_general x9, matrix products: 11.9 us -> 4.35 us  [on_device(): lax.dot_general(piece, dpre, dims, preferred_element_type=jnp.float32)]
  transfers between devices with their start and end apart: 7 -> 7, of which waited for: 4 -> 4; matrix products, arithmetic and copies ran while one was open for 12% -> 18% of each run, Pallas kernels for 0% -> 0%
where the time goes in v1:
time: 320 us; the launch traced here: 319 us
  waiting for transfers between devices  222 us (69%)
  matrix products  52.1 us (16%)
  between operations  15.6 us (5%)
  other arithmetic  14.9 us (5%)
  local copies, waits for them, and re-layouts  9.43 us (3%)
  starting transfers between devices  5.1 us (2%)
    psum x1, waiting for transfers between devices, on_device(): lax.psum((spatial_terms, temporal_terms, cond_terms), ('space', 'tm'))  101 us
    psum x1, waiting for transfers between devices, on_device(): cot_sum = lax.psum(jnp.sum(cot, axis=1, dtype=jnp.float32), 'space')  61 us
    ppermute x2, waiting for transfers between devices, shifted(): return lax.ppermute(value, axis, pairs)  60.3 us
    dot_general x18, matrix products, spatial_sum(): total = total + jnp.dot(piece, kernel, preferred_element_type=jnp.float32)  28.7 us
    dot_general x3, matrix products, lag_backward(): jnp.dot(padded_cot[:, lag:lag + count], weights[lag].T, preferred_element...  6.59 us
  transfers between devices with their start and end apart: 7, of which 4 were waited for; matrix products, arithmetic and copies ran while one was open for 18% of the time, Pallas kernels for 0%

profile of v1, /device:TPU:0, one launch (start us, length us, event | category | flops | bytes accessed | tf_op | source)
XLA Modules:
  0.0 319.5 jit_solution(17368801483664651873)
XLA Ops:
  8.1 0.8 fusion.123
  8.9 2.3 broadcast_multiply_fusion.1
  11.3 1.4 convert_reduce_fusion
  12.7 1.3 collective-permute-start.1
  14.1 1.8 fusion.74
  15.9 28.7 %collective-permute-done.1 = bf16[2,2,2,256,256]{4,3,2,1,0:T(8,128)(2,1)S(1)} collective-permute-done((bf16[2,2,2,256,256]{4,3,2,1,0:T(8,128)(2,1)S(1)}, bf16[2,2,2,256,256]{4,3,2,1,0:T(8,128)(2,1)S(1)}, u32[]{:S(2)}, u32[]{:S(2)}) %collective-permute-start.1) | collective-permute-done | bytes 1048608 | tf_op jit(solution)/shard_map/ppermute | solution.py:19
  44.6 1.0 copy-done.22
  45.5 1.8 fusion.3
  47.4 1.8 pad_dynamic-slice_fusion.1
  52.8 2.2 multiply_convert_fusion.3
  55.7 3.0 multiply_convert_fusion.1
  58.7 2.0 slice_select_fusion
  60.8 61.0 %all-reduce.8.cloned.1.call-done = f32[2,2,256,256]{3,2,1,0:T(8,128)} async-done(((f32[2,2,256,256]{3,2,1,0:T(8,128)}), f32[2,2,256,256]{3,2,1,0:T(8,128)}) %all-reduce.8.cloned.1.call-update) | async-done | bytes 1048592 | tf_op jit(solution)/shard_map/psum | solution.py:105
  121.8 2.9 fusion.44
  124.7 3.6 %collective-permute-start = (bf16[2,2,2,256,256]{4,3,2,1,0:T(8,128)(2,1)S(1)}, bf16[2,2,2,256,256]{4,3,2,1,0:T(8,128)(2,1)S(1)}, u32[]{:S(2)}, u32[]{:S(2)}) collective-permute-start(bf16[2,2,2,256,256]{4,3,2,1,0:T(8,128)(2,1)S(1)} %copy-done.5), channel_id=1, source_target_pairs={{0,2},{2,4},{4,6},{6,8},{8,10},{10,12},{12,14},{1,3},{3,5},{5,7},{... | collective-permute-start | bytes 3145736 | tf_op jit(solution)/shard_map/ppermute | solution.py:19
  128.9 0.5 fusion.12
  129.3 0.5 fusion.18
  129.8 0.5 fusion.17
  130.8 0.5 fusion.16
  131.3 0.5 fusion.15
  131.8 0.7 copy-done.3
  133.0 0.5 fusion.10
  133.5 0.5 fusion.14
  134.0 0.5 copy-done.20
  134.5 2.1 fusion.76
  136.6 31.6 %collective-permute-done = bf16[2,2,2,256,256]{4,3,2,1,0:T(8,128)(2,1)S(1)} collective-permute-done((bf16[2,2,2,256,256]{4,3,2,1,0:T(8,128)(2,1)S(1)}, bf16[2,2,2,256,256]{4,3,2,1,0:T(8,128)(2,1)S(1)}, u32[]{:S(2)}, u32[]{:S(2)}) %collective-permute-start) | collective-permute-done | bytes 1048608 | tf_op jit(solution)/shard_map/ppermute | solution.py:19
  169.1 1.0 pad_maximum_fusion.5
  170.1 1.7 fusion.7
  171.8 1.8 pad_dynamic-slice_fusion
  173.6 1.9 fusion.20
  175.5 1.8 fusion.22
  177.3 1.8 fusion.24
  179.1 1.8 fusion.26
  180.9 1.8 fusion.28
  182.8 1.9 fusion.30
  184.7 1.8 fusion.56
  186.5 1.8 fusion.64
  188.3 2.9 bitcast_reduce_fusion
  191.2 0.8 copy-done.11
  192.0 1.5 fusion.13
  193.5 1.2 copy-done.4
  194.7 8.4 %fusion.2 = bf16[2,2,2,256,256]{4,3,2,1,0:T(8,128)(2,1)} fusion(bf16[2,2,2,256,256]{4,3,2,1,0:T(8,128)(2,1)S(1)} %copy-done.4, f32[2,2,2,256,256]{4,3,2,1,0:T(8,128)} %fusion.20, f32[2,2,2,256,256]{4,3,2,1,0:T(8,128)} %fusion.22, f32[2,2,2,256,256]{4,3,2,1,0:T(8,128)} %fusion.24, f32[2,2,2,256,256]{4,3,2,1,0:T(8,128)} %fusion.56, ...), kind=kOutput, calls=%fused_computation.8 | convolution fusion | flops 275775488 | bytes 22151192 | tf_op jit(solution)/shard_map/dot_general | solution.py:36
  203.4 0.9 copy-done.7
  204.3 2.6 multiply_convert_fusion.2
  206.8 101.0 %all-reduce.10.cloned.1.call-done = (f32[9,256,256]{2,1,0:T(8,128)}, f32[3,256,256]{2,1,0:T(8,128)}, f32[256,256]{1,0:T(8,128)}) async-done(((f32[9,256,256]{2,1,0:T(8,128)}, f32[3,256,256]{2,1,0:T(8,128)}, f32[256,256]{1,0:T(8,128)}), (f32[9,256,256]{2,1,0:T(8,128)}, f32[3,256,256]{2,1,0:T(8,128)}, f32[256,256]{1,0:T(8,128)})) %all-reduce.10.cloned.1.call-update) | async-done | bytes 3407888 | tf_op jit(solution)/shard_map/psum | solution.py:130
  307.8 3.0 multiply_convert_fusion
  310.9 0.8 multiply_convert_fusion.4
  311.7 0.7 multiply_convert_fusion.5
  (75 shorter events, 7.4 us)
Async XLA Ops:
  8.0 113.8 %copy-start = (bf16[256,256]{1,0:T(8,128)(2,1)S(1)}, bf16[256,256]{1,0:T(8,128)(2,1)}, u32[]{:S(2)}) copy-start(bf16[256,256]{1,0:T(8,128)(2,1)} %param.11) | copy-start | bytes 393220
  8.0 3.3 %copy-start.21 = (bf16[2,2,2,256,256]{4,3,2,1,0:T(8,128)(2,1)S(1)}, bf16[2,2,2,256,256]{4,3,2,1,0:T(8,128)(2,1)}, u32[]{:S(2)}) copy-start(bf16[2,2,2,256,256]{4,3,2,1,0:T(8,128)(2,1)} %param.7) | copy-start | bytes 3145732
  8.0 39.4 %all-gather.5.cloned.1.call-start = ((), (), s32[]{:S(2)}) async-start(), calls=%async_computation | async-start | bytes 3145728 | tf_op jit(solution)/shard_map/all_gather | solution.py:89
  11.3 2.8 copy-start.19
  11.3 110.6 %all-reduce.8.cloned.1.call-start = ((), (), s32[]{:S(2)}) async-start(), calls=%async_computation.2 | async-start | bytes 2097152 | tf_op jit(solution)/shard_map/psum | solution.py:105
  12.7 31.9 %copy-start.2 = (bf16[2,2,2,256,256]{4,3,2,1,0:T(8,128)(2,1)}, bf16[2,2,2,256,256]{4,3,2,1,0:T(8,128)(2,1)S(1)}, u32[]{:S(2)}) copy-start(bf16[2,2,2,256,256]{4,3,2,1,0:T(8,128)(2,1)S(1)} %get-tuple-element.9) | copy-start | bytes 3145732
  12.7 31.8 %collective-permute-start.1 = (bf16[2,2,2,256,256]{4,3,2,1,0:T(8,128)(2,1)S(1)}, bf16[2,2,2,256,256]{4,3,2,1,0:T(8,128)(2,1)S(1)}, u32[]{:S(2)}, u32[]{:S(2)}) collective-permute-start(bf16[2,2,2,256,256]{4,3,2,1,0:T(8,128)(2,1)S(1)} %get-tuple-element.9), channel_id=1, source_target_pairs={{2,0},{4,2},{6,4},{8,6},{10,8},{12,10},{14,12},{3,1},{5,3},{7,5},{... | collective-permute-start | bytes 3145736 | tf_op jit(solution)/shard_map/ppermute | solution.py:19
  14.0 157.8 %all-gather.7.cloned.1.call-start = ((), (), s32[]{:S(2)}) async-start(), calls=%async_computation.1 | async-start | bytes 3145728 | tf_op jit(solution)/shard_map/all_gather | solution.py:107
  44.6 1.0 copy-start.22
  47.4 1.8 copy-start.13
  52.7 2.2 copy-start.17
  52.8 2.6 copy-start.18
  52.8 2.9 copy-start.23
  58.7 69.7 %copy-start.1 = (bf16[2,2,2,256,256]{4,3,2,1,0:T(8,128)(2,1)S(1)}, bf16[2,2,2,256,256]{4,3,2,1,0:T(8,128)(2,1)}, u32[]{:S(2)}) copy-start(bf16[2,2,2,256,256]{4,3,2,1,0:T(8,128)(2,1)} %multiply_convert_fusion.1) | copy-start | bytes 3145732
  58.7 129.6 %all-gather.9.cloned.1.call-start = ((), (), s32[]{:S(2)}) async-start(), calls=%async_computation.3 | async-start | bytes 4718592 | tf_op jit(solution)/shard_map/all_gather | solution.py:8
  60.8 247.1 %all-reduce.10.cloned.1.call-start = ((), (), s32[]{:S(2)}) async-start(), calls=%async_computation.4 | async-start | bytes 6815744 | tf_op jit(solution)/shard_map/psum | solution.py:130
  121.8 2.9 copy-start.5
  124.7 43.4 %collective-permute-start = (bf16[2,2,2,256,256]{4,3,2,1,0:T(8,128)(2,1)S(1)}, bf16[2,2,2,256,256]{4,3,2,1,0:T(8,128)(2,1)S(1)}, u32[]{:S(2)}, u32[]{:S(2)}) collective-permute-start(bf16[2,2,2,256,256]{4,3,2,1,0:T(8,128)(2,1)S(1)} %copy-done.5), channel_id=1, source_target_pairs={{0,2},{2,4},{4,6},{6,8},{8,10},{10,12},{12,14},{1,3},{3,5},{5,7},{... | collective-permute-start | bytes 3145736 | tf_op jit(solution)/shard_map/ppermute | solution.py:19
  131.3 1.2 copy-start.3
  133.5 1.0 copy-start.20
  134.5 34.1 %copy-start.16 = (f32[9,256,256]{2,1,0:T(8,128)}, f32[9,256,256]{2,1,0:T(8,128)S(1)}, u32[]{:S(2)}) copy-start(f32[9,256,256]{2,1,0:T(8,128)S(1)} %fusion.14) | copy-start | bytes 7077892
  168.2 1.9 copy-start.6
  171.8 1.8 copy-start.14
  188.3 3.7 %copy-start.15 = (f32[2,2,256,256]{3,2,1,0:T(8,128)S(1)}, f32[2,2,256,256]{3,2,1,0:T(8,128)}, u32[]{:S(2)}) copy-start(f32[2,2,256,256]{3,2,1,0:T(8,128)} %all-reduce.8.cloned.1.call-done) | copy-start | bytes 3145732
  191.2 0.8 copy-start.11
  193.5 1.2 copy-start.4
  194.7 8.4 %copy-start.12 = (bf16[2,2,256,256]{3,2,1,0:T(8,128)(2,1)S(1)}, bf16[2,2,256,256]{3,2,1,0:T(8,128)(2,1)}, u32[]{:S(2)}) copy-start(bf16[2,2,256,256]{3,2,1,0:T(8,128)(2,1)} %copy-done.11) | copy-start | bytes 1572868
  194.7 8.7 %copy-start.8 = (bf16[2,2,2,256,256]{4,3,2,1,0:T(8,128)(2,1)S(1)}, bf16[2,2,2,256,256]{4,3,2,1,0:T(8,128)(2,1)}, u32[]{:S(2)}) copy-start(bf16[2,2,2,256,256]{4,3,2,1,0:T(8,128)(2,1)} %broadcast_multiply_fusion.1) | copy-start | bytes 3145732
  194.7 8.7 %copy-start.9 = (f32[2,2,2,256,256]{4,3,2,1,0:T(8,128)S(1)}, f32[2,2,2,256,256]{4,3,2,1,0:T(8,128)}, u32[]{:S(2)}) copy-start(f32[2,2,2,256,256]{4,3,2,1,0:T(8,128)} %fusion.76) | copy-start | bytes 6291460
  194.7 8.7 %copy-start.10 = (f32[2,2,2,256,256]{4,3,2,1,0:T(8,128)S(1)}, f32[2,2,2,256,256]{4,3,2,1,0:T(8,128)}, u32[]{:S(2)}) copy-start(f32[2,2,2,256,256]{4,3,2,1,0:T(8,128)} %fusion.7) | copy-start | bytes 6291460
  203.0 1.2 copy-start.7
  307.8 3.0 copy-start.24
  307.8 3.9 %copy-start.25 = (f32[256,256]{1,0:T(8,128)S(1)}, f32[256,256]{1,0:T(8,128)}, u32[]{:S(2)}) copy-start(f32[256,256]{1,0:T(8,128)} %get-tuple-element.7) | copy-start | bytes 786436
Sparse Core Ops, SparseCore 0:
  11.4 13.2 all-gather.4
  58.8 19.3 all-gather.6
  80.3 98.8 all-gather.8
Sparse Core Ops, SparseCore 1:
  15.8 106.0 all-reduce.7
  193.6 114.2 all-reduce.9
